TPU v7x, 128 devices: a whole 4x4x4 slice. The times are simulated.
128 devices in a mesh: group: 16 (over x, z), mp: 8 (over y, core).
Axes of the slice: x: 4, y: 4, z: 4, core: 2. Of those that a mesh axis runs over, the one named last changes fastest.
Arguments:
- stream: bfloat16 [8192, 3584], P('group', 'mp'), may hold values from -6 to 6
- prenorm_gain: float32 [3584], replicated, may hold values from 0.25 to 12
- query_weight: bfloat16 [3584, 4096], P(None, 'mp'), may hold values from -0.09375 to 0.09375
- key_weight: bfloat16 [3584, 2048], P(None, 'mp'), may hold values from -0.09375 to 0.09375
- value_weight: bfloat16 [3584, 2048], P(None, 'mp'), may hold values from -0.09375 to 0.09375
- output_weight: bfloat16 [4096, 3584], P('mp'), may hold values from -0.09375 to 0.09375
- adapter_down_rows: bfloat16 [64, 16, 3584], P('group', None, 'mp'), may hold values from -0.09375 to 0.09375
- adapter_up_query: bfloat16 [64, 16, 4096], P('group', None, 'mp'), may hold values from -1.5 to 1.5
- request_adapter: int32 [16, 4], replicated, may hold values from 0 to 63
- adapter_row_index: int32 [64], replicated, may hold values from 0 to 63, each once
- request_token_length: int32 [16, 4], replicated, may hold values from 1 to 256, 512 in all within a row
- continues_previous: int32 [16], replicated, may hold values from 0 to 1, as said below
- request_cache_block: int32 [16, 4], replicated, may hold values from 0 to 31, as said below
- cached_length: int32 [16, 4], replicated, may hold values from 1 to 256
- cached_rotated_keys: bfloat16 [32, 256, 2048], P('group', None, 'mp'), may hold values from -6 to 6
- cached_value_rows: bfloat16 [32, 256, 2048], P('group', None, 'mp'), may hold values from -6 to 6
Outputs:
- attn_out: bfloat16 [8192, 3584], P('group', 'mp')
Inputs may be any that keep to these rules, and one draw needn't show every extreme that they name: `continues_previous`: the first group has 0; some group has 1. `request_cache_block`: the owner of block b is group b // 2; blocks may be shared by requests.
All inputs are finite; a program needn't handle non-finite values.
Results may differ from a plain program's by a relative error of at most 0.017.
The roundings to bfloat16 on the way count: a program that leaves them out, or rounds other values in their place, can miss the bound.
Values may be sent and summed in bfloat16 or wider, within the bound.
No kernel may reach another device: no remote copies, remote signals or barrier semaphores. Data moves between devices by JAX's collectives and lax.ppermute only.
A program may use at most 128 MiB of HBM per device.

v0:
```python
import jax
import jax.numpy as jnp
from jax import lax
from jax.sharding import PartitionSpec as P

HEAD_WIDTH = 256
REQS = 4
adapter_scale = 2.0


def shifted(value, axis, steps):
    count = lax.axis_size(axis)
    first, last = (max(0, -steps), min(count, count - steps))
    return lax.ppermute(value, axis, [(source, source + steps) for source in range(first, last)])


def rotate(values, position, head_size):
    count = values.shape[0]
    shaped = values.reshape(count, -1, head_size)
    half = head_size // 2
    freq = 10000.0 ** (-jnp.arange(half, dtype=jnp.float32) / half)
    angle = position[:, None, None] * freq[None, None, :]
    cosine = jnp.cos(angle)
    sine = jnp.sin(angle)
    first = shaped[..., :half]
    second = shaped[..., half:]
    turned = jnp.concatenate(
        [first * cosine - second * sine, second * cosine + first * sine], axis=-1
    )
    return turned.reshape(count, -1)


def layout(lengths, cached, split_flag, prev_len, count):
    ends = jnp.cumsum(lengths)
    starts = ends - lengths
    place = jnp.arange(count, dtype=jnp.int32)
    member = ((place[:, None] >= starts[None, :]) & (place[:, None] < ends[None, :])).astype(
        jnp.int32
    )
    request = jnp.sum(member * jnp.arange(lengths.shape[0], dtype=jnp.int32)[None, :], axis=1)
    offset = place - jnp.sum(member * starts[None, :], axis=1)
    extra = jnp.where(request == 0, split_flag * prev_len, 0)
    position = jnp.sum(member * cached[None, :], axis=1) + extra + offset
    return (member, request, position.astype(jnp.float32))


def attend(
    query_vectors,
    keys,
    values,
    prev_keys,
    prev_values,
    cache_keys,
    cache_values,
    request,
    cached,
    split_flag,
    prev_len,
    head_size,
):
    count = query_vectors.shape[0]
    kv_heads = keys.shape[1] // head_size
    ratio = query_vectors.shape[1] // keys.shape[1]
    block = cache_keys.shape[1]
    slots = cache_keys.shape[0] * block
    every_key = jnp.concatenate([cache_keys.reshape(slots, -1), prev_keys, keys], 0).reshape(
        -1, kv_heads, head_size
    )
    every_value = jnp.concatenate(
        [cache_values.reshape(slots, -1), prev_values, values], 0
    ).reshape(-1, kv_heads, head_size)
    slot_req = jnp.arange(slots, dtype=jnp.int32) // block
    slot_col = jnp.arange(slots, dtype=jnp.int32) % block
    cache_ok = (request[:, None] == slot_req[None, :]) & (
        slot_col[None, :] < cached[slot_req][None, :]
    )
    place = jnp.arange(count, dtype=jnp.int32)
    prev_ok = (split_flag == 1) & (request[:, None] == 0) & (place[None, :] >= count - prev_len)
    own_ok = (request[:, None] == request[None, :]) & (place[None, :] <= place[:, None])
    allowed = jnp.concatenate([cache_ok, prev_ok, own_ok], 1)
    grouped = query_vectors.reshape(count, kv_heads, ratio, head_size)
    scores = jnp.einsum(
        "tkrd,skd->krts", grouped, every_key, preferred_element_type=jnp.float32
    ) * head_size ** (-0.5)
    scores = jnp.where(allowed[None, None], scores, jnp.float32(-1e30))
    top = jnp.max(scores, axis=-1, keepdims=True)
    weights = jnp.exp(scores - top)
    total = jnp.sum(weights, axis=-1)
    numer = jnp.einsum(
        "krts,skd->tkrd",
        weights.astype(jnp.bfloat16),
        every_value,
        preferred_element_type=jnp.float32,
    )
    result = numer / jnp.transpose(total, (2, 0, 1))[..., None]
    return result.reshape(count, -1).astype(jnp.bfloat16)


def on_device(
    stream,
    prenorm_gain,
    query_weight,
    key_weight,
    value_weight,
    output_weight,
    adapter_down_rows,
    adapter_up_query,
    request_adapter,
    adapter_row_index,
    request_token_length,
    continues_previous,
    request_cache_block,
    cached_length,
    cached_rotated_keys,
    cached_value_rows,
):
    count = stream.shape[0]
    width = stream.shape[1]
    group_at = lax.axis_index("group")
    model_at = lax.axis_index("mp")
    whole = lax.all_gather(stream, "mp", axis=1, tiled=True)
    wide = whole.astype(jnp.float32)
    normalized_input = (
        wide * lax.rsqrt(jnp.mean(wide * wide, axis=1, keepdims=True) + 1e-06) * prenorm_gain
    ).astype(jnp.bfloat16)
    normed_part = lax.dynamic_slice_in_dim(normalized_input, model_at * width, width, 1)
    before = jnp.maximum(group_at - 1, 0)
    lengths = request_token_length[group_at]
    cached = cached_length[group_at]
    split_flag = continues_previous[group_at]
    prev_len = request_token_length[before, REQS - 1]
    member, request, position = layout(lengths, cached, split_flag, prev_len, count)
    wanted = adapter_row_index[request_adapter[group_at]]
    pieces = (
        lax.all_gather(adapter_down_rows, "group", axis=0, tiled=True),
        lax.all_gather(adapter_up_query, "group", axis=0, tiled=True),
    )
    stored = jnp.arange(pieces[0].shape[0], dtype=jnp.int32)
    onehot = (wanted[:, None] == stored[None, :]).astype(jnp.bfloat16)
    new_down = jnp.einsum("rj,jkd->rkd", onehot, pieces[0], preferred_element_type=jnp.float32)
    new_up = jnp.einsum("rj,jkd->rkd", onehot, pieces[1], preferred_element_type=jnp.float32)
    chosen_down = new_down.astype(jnp.bfloat16)
    chosen_up = new_up.astype(jnp.bfloat16)
    rank_index = adapter_down_rows.shape[1]
    partial_low = jnp.einsum(
        "td,rkd->trk", normed_part, chosen_down, preferred_element_type=jnp.float32
    ).reshape(count, REQS * rank_index)
    low = lax.psum(partial_low, "mp").astype(jnp.bfloat16)
    own_columns = jnp.repeat(member, rank_index, axis=1).astype(jnp.bfloat16)
    query_update = jnp.dot(
        low * own_columns,
        chosen_up.reshape(REQS * rank_index, -1),
        preferred_element_type=jnp.float32,
    )
    query_vectors = (
        jnp.dot(normalized_input, query_weight, preferred_element_type=jnp.float32)
        + adapter_scale * query_update
    )
    query_vectors = rotate(query_vectors, position, HEAD_WIDTH).astype(jnp.bfloat16)
    keys = rotate(
        jnp.dot(normalized_input, key_weight, preferred_element_type=jnp.float32),
        position,
        HEAD_WIDTH,
    ).astype(jnp.bfloat16)
    values = jnp.dot(normalized_input, value_weight, preferred_element_type=jnp.float32).astype(
        jnp.bfloat16
    )
    prev_keys, prev_values = shifted((keys, values), "group", 1)
    blocks = request_cache_block[group_at]
    pieces = (
        lax.all_gather(cached_rotated_keys, "group", axis=0, tiled=True),
        lax.all_gather(cached_value_rows, "group", axis=0, tiled=True),
    )
    stored = jnp.arange(pieces[0].shape[0], dtype=jnp.int32)
    onehot = (blocks[:, None] == stored[None, :]).astype(jnp.bfloat16)
    new_keys = jnp.einsum("rj,jcd->rcd", onehot, pieces[0], preferred_element_type=jnp.float32)
    new_values = jnp.einsum("rj,jcd->rcd", onehot, pieces[1], preferred_element_type=jnp.float32)
    cache_keys = new_keys.astype(jnp.bfloat16)
    cache_values = new_values.astype(jnp.bfloat16)
    attended = attend(
        query_vectors,
        keys,
        values,
        prev_keys,
        prev_values,
        cache_keys,
        cache_values,
        request,
        cached,
        split_flag,
        prev_len,
        HEAD_WIDTH,
    )
    partial_out = jnp.dot(attended, output_weight, preferred_element_type=jnp.float32)
    return lax.psum_scatter(partial_out.astype(jnp.bfloat16), "mp", scatter_dimension=1, tiled=True)


def solution(mesh):
    placed = (
        P("group", "mp"),
        P(),
        P(None, "mp"),
        P(None, "mp"),
        P(None, "mp"),
        P("mp", None),
        P("group", None, "mp"),
        P("group", None, "mp"),
        P(),
        P(),
        P(),
        P(),
        P(),
        P(),
        P("group", None, "mp"),
        P("group", None, "mp"),
    )
    return jax.shard_map(
        on_device, mesh=mesh, in_specs=placed, out_specs=P("group", "mp"), check_vma=False
    )
```

profile of v0, /device:TPU:0, one launch (start us, length us, event | category | flops | bytes accessed | tf_op | source)
XLA Modules:
  0.0 254.0 jit_solution(16617972660007501374)
XLA Ops:
  13.4 26.9 %all_gather.18 = bf16[64,16,448]{2,1,0:T(8,128)(2,1)S(1)} all-gather(bf16[4,16,448]{2,1,0:T(8,128)(2,1)} %param.22), channel_id=1, replica_groups=mesh['group'=16,'mp'=8] {'group'}, dimensions={0}, use_global_device_ids=true | all-gather | bytes 974848 | tf_op jit(solution)/shard_map/all_gather | solution.py:135
  40.9 2.6 %compare_select_fusion.1 = s32[1024,1]{0,1:T(1,128)S(1)} fusion(s32[]{:T(128)} %bitcast.7, s32[]{:T(128)} %bitcast.8, s32[]{:T(128)} %bitcast.10, s32[]{:T(128)} %bitcast.9), kind=kLoop, calls=%fused_computation.71 | loop fusion | flops 17408 | bytes 4112 | tf_op jit(solution)/shard_map/gather | solution.py:75
  49.5 1.8 multiply_cosine_fusion
  54.9 2.4 convolution_convert_fusion.2
  57.4 28.5 %all-gather.7.cloned.1.call-done = bf16[512,3584]{0,1:T(8,128)(2,1)} async-done(((bf16[512,448]{0,1:T(8,128)(2,1)}), bf16[512,3584]{0,1:T(8,128)(2,1)}) %all-gather.7.cloned.1.call-update) | async-done | bytes 3670032 | tf_op jit(solution)/shard_map/all_gather | solution.py:121
  85.8 3.0 %fusion.2 = f32[512]{0:T(512)S(1)} fusion(bf16[512,3584]{0,1:T(8,128)(2,1)} %all-gather.7.cloned.1.call-done), kind=kLoop, calls=%fused_computation.7 | loop fusion | flops 5504512 | bytes 3672064 | tf_op jit(solution)/shard_map/reduce_sum | solution.py:124
  90.6 1.8 copy-done.2
  92.4 1.9 convolution_convert_fusion.1
  96.1 4.2 %collective-permute-start = (bf16[512,256]{1,0:T(8,128)(2,1)}, bf16[512,256]{1,0:T(8,128)(2,1)}, u32[]{:S(2)}, u32[]{:S(2)}) collective-permute-start(bf16[512,256]{1,0:T(8,128)(2,1)} %convolution_convert_fusion.1), channel_id=1, source_target_pairs={{0,8},{8,16},{16,24},{24,32},{32,40},{40,48},{48,56},{56,64},{64,7... | collective-permute-start | bytes 786440 | tf_op jit(solution)/shard_map/ppermute | solution.py:14
  100.2 3.8 %convolution_bitcast_fusion = f32[512,1,256]{0,2,1:T(8,128)S(1)} fusion(bf16[512,3584]{0,1:T(8,128)(2,1)} %copy-done.2, bf16[3584,256]{1,0:T(8,128)(2,1)} %param.19), kind=kOutput, calls=%fused_computation.26 | convolution fusion | flops 939524096 | bytes 6029312 | tf_op jit(solution)/shard_map/dot_general | solution.py:161
  107.7 3.4 %collective-permute-start.1 = (bf16[512,256]{0,1:T(8,128)(2,1)}, bf16[512,256]{0,1:T(8,128)(2,1)}, u32[]{:S(2)}, u32[]{:S(2)}) collective-permute-start(bf16[512,256]{0,1:T(8,128)(2,1)} %maximum_bitcast_fusion.6), channel_id=1, source_target_pairs={{0,8},{8,16},{16,24},{24,32},{32,40},{40,48},{48,56},{56,64},{64,7... | collective-permute-start | bytes 786440 | tf_op jit(solution)/shard_map/ppermute | solution.py:14
  112.3 26.0 %all-reduce.1 = bf16[512,64]{0,1:T(8,128)(2,1)S(1)} all-reduce(f32[512,64]{0,1:T(8,128)S(1)} %bitcast.101), channel_id=1, replica_groups=mesh['group'=16,'mp'=8] {'mp'}, use_global_device_ids=true, to_apply=%region_5.6 | all-reduce | flops 32768 | bytes 196608 | tf_op jit(solution)/shard_map/psum | solution.py:148
  138.4 5.3 %fusion.82 = f32[512,512]{0,1:T(8,128)S(1)} fusion(bf16[512,3584]{0,1:T(8,128)(2,1)} %copy-done.2, bf16[3584,512]{1,0:T(8,128)(2,1)} %param.18), kind=kOutput, calls=%fused_computation.129 | convolution fusion | flops 1879048192 | bytes 8388608 | tf_op jit(solution)/shard_map/dot_general | solution.py:156
  146.4 2.1 copy.62
  148.5 2.2 subtract_convert_fusion
  150.6 1.8 copy.46
  154.3 4.6 %fusion.18 = bf16[4,256,256]{2,0,1:T(4,128)(2,1)S(1)} fusion(bf16[32,256,256]{2,1,0:T(8,128)(2,1)} %all-gather.5.cloned.1.call-done, s32[4]{0:T(128)S(1)} %dynamic-slice_reduce_fusion.1), kind=kOutput, calls=%fused_computation.24 | convolution fusion | flops 17039488 | bytes 4718608 | tf_op jit(solution)/shard_map/rj,jcd->rcd/dot_general | solution.py:177
  160.0 35.3 %all-gather.9.cloned.1.call-done = bf16[32,256,256]{2,1,0:T(8,128)(2,1)} async-done(((bf16[2,256,256]{2,1,0:T(8,128)(2,1)}), bf16[32,256,256]{2,1,0:T(8,128)(2,1)}) %all-gather.9.cloned.1.call-update) | async-done | bytes 4194320 | tf_op jit(solution)/shard_map/all_gather | solution.py:171
  195.3 4.7 %fusion.21 = bf16[4,256,256]{2,0,1:T(4,128)(2,1)S(1)} fusion(bf16[32,256,256]{2,1,0:T(8,128)(2,1)} %all-gather.9.cloned.1.call-done, s32[4]{0:T(128)S(1)} %dynamic-slice_reduce_fusion.1), kind=kOutput, calls=%fused_computation.25 | convolution fusion | flops 17039488 | bytes 4718608 | tf_op jit(solution)/shard_map/rj,jcd->rcd/dot_general | solution.py:176
  200.1 1.8 fusion.5
  201.9 2.2 fusion
  204.2 2.8 %divide_convert_fusion = bf16[512,1,2,256]{0,3,2,1:T(8,128)(2,1)S(1)} fusion(f32[2048,512,2]{1,0,2:T(8,128)S(1)} %get-tuple-element.25, f32[2,512]{1,0:T(2,128)S(1)} %get-tuple-element.24, pred[512,2048]{0,1:T(8,128)(4,1)S(1)} %pad_add_fusion, bf16[512,256]{0,1:T(8,128)(2,1)S(1)} %copy-done.4, bf16[512,256]{0,1:T(8,128)(2,1)S(1)} %copy-done.6, ...), kind=kOutput, calls=%fused_computation.43 | convolution fusion | flops 1085800448 | bytes 11018240 | tf_op jit(solution)/shard_map/krts,skd->tkrd/dot_general | solution.py:89
  207.0 3.9 %convolution_convert_fusion = bf16[512,3584]{0,1:T(8,128)(2,1)} fusion(bf16[512,512]{0,1:T(8,128)(2,1)S(1)} %bitcast.107, bf16[512,3584]{1,0:T(8,128)(2,1)S(1)} %copy-done.11), kind=kOutput, calls=%fused_computation.11 | convolution fusion | flops 1880883200 | bytes 7864320 | tf_op jit(solution)/shard_map/dot_general | solution.py:194
  210.9 36.5 %reduce-scatter.2.cloned.1.call-done = bf16[512,448]{0,1:T(8,128)(2,1)} async-done(((bf16[512,3584]{0,1:T(8,128)(2,1)}), bf16[512,448]{0,1:T(8,128)(2,1)}) %reduce-scatter.2.cloned.1.call-update) | async-done | bytes 458768 | tf_op jit(solution)/shard_map/reduce_scatter | solution.py:195
  (78 shorter events, 28.4 us)
Async XLA Ops:
  6.5 85.8 %copy-start = (bf16[3584,256]{1,0:T(8,128)(2,1)S(1)}, bf16[3584,256]{1,0:T(8,128)(2,1)}, u32[]{:S(2)}) copy-start(bf16[3584,256]{1,0:T(8,128)(2,1)} %param.20) | copy-start | bytes 5505028
  6.5 48.4 %all-gather.11.cloned.1.call-start = ((), (), s32[]{:S(2)}) async-start(), calls=%async_computation.4 | async-start | bytes 1114112 | tf_op jit(solution)/shard_map/all_gather | solution.py:136
  7.3 78.6 %all-gather.7.cloned.1.call-start = ((), (), s32[]{:S(2)}) async-start(), calls=%async_computation.2 | async-start | bytes 4128768 | tf_op jit(solution)/shard_map/all_gather | solution.py:121
  8.0 146.3 %all-gather.5.cloned.1.call-start = ((), (), s32[]{:S(2)}) async-start(), calls=%async_computation.1 | async-start | bytes 4456448 | tf_op jit(solution)/shard_map/all_gather | solution.py:172
  8.7 186.5 %all-gather.9.cloned.1.call-start = ((), (), s32[]{:S(2)}) async-start(), calls=%async_computation.3 | async-start | bytes 4456448 | tf_op jit(solution)/shard_map/all_gather | solution.py:171
  9.3 238.1 %reduce-scatter.2.cloned.1.call-start = ((), (), s32[]{:S(2)}) async-start(), calls=%async_computation.5 | async-start | bytes 4128768 | tf_op jit(solution)/shard_map/reduce_scatter | solution.py:195
  53.4 35.5 %copy-start.10 = (f32[3584]{0:T(1024)S(1)}, f32[3584]{0:T(1024)}, u32[]{:S(2)}) copy-start(f32[3584]{0:T(1024)} %param.17) | copy-start | bytes 43012
  85.8 3.1 %copy-start.1 = (bf16[512,3584]{0,1:T(8,128)(2,1)S(1)}, bf16[512,3584]{0,1:T(8,128)(2,1)}, u32[]{:S(2)}) copy-start(bf16[512,3584]{0,1:T(8,128)(2,1)} %all-gather.7.cloned.1.call-done) | copy-start | bytes 11010052
  90.5 1.8 copy-start.2
  96.1 54.6 %collective-permute-start = (bf16[512,256]{1,0:T(8,128)(2,1)}, bf16[512,256]{1,0:T(8,128)(2,1)}, u32[]{:S(2)}, u32[]{:S(2)}) collective-permute-start(bf16[512,256]{1,0:T(8,128)(2,1)} %convolution_convert_fusion.1), channel_id=1, source_target_pairs={{0,8},{8,16},{16,24},{24,32},{32,40},{40,48},{48,56},{56,64},{64,7... | collective-permute-start | bytes 786440 | tf_op jit(solution)/shard_map/ppermute | solution.py:14
  107.7 44.8 %collective-permute-start.1 = (bf16[512,256]{0,1:T(8,128)(2,1)}, bf16[512,256]{0,1:T(8,128)(2,1)}, u32[]{:S(2)}, u32[]{:S(2)}) collective-permute-start(bf16[512,256]{0,1:T(8,128)(2,1)} %maximum_bitcast_fusion.6), channel_id=1, source_target_pairs={{0,8},{8,16},{16,24},{24,32},{32,40},{40,48},{48,56},{56,64},{64,7... | collective-permute-start | bytes 786440 | tf_op jit(solution)/shard_map/ppermute | solution.py:14
  160.0 40.1 %copy-start.5 = (bf16[512,256]{1,0:T(8,128)(2,1)S(1)}, bf16[512,256]{1,0:T(8,128)(2,1)}, u32[]{:S(2)}) copy-start(bf16[512,256]{1,0:T(8,128)(2,1)} %copy.52) | copy-start | bytes 786436
  160.0 40.1 %copy-start.7 = (bf16[512,256]{1,0:T(8,128)(2,1)S(1)}, bf16[512,256]{1,0:T(8,128)(2,1)}, u32[]{:S(2)}) copy-start(bf16[512,256]{1,0:T(8,128)(2,1)} %copy.51) | copy-start | bytes 786436
  195.3 4.8 %copy-start.8 = (bf16[512,2,128]{2,0,1:T(8,128)(2,1)S(1)}, bf16[512,2,128]{2,0,1:T(8,128)(2,1)}, u32[]{:S(2)}) copy-start(bf16[512,2,128]{2,0,1:T(8,128)(2,1)} %get-tuple-element.12) | copy-start | bytes 786436
  195.3 4.8 %copy-start.9 = (bf16[512,2,128]{2,0,1:T(8,128)(2,1)S(1)}, bf16[512,2,128]{2,0,1:T(8,128)(2,1)}, u32[]{:S(2)}) copy-start(bf16[512,2,128]{2,0,1:T(8,128)(2,1)} %get-tuple-element.13) | copy-start | bytes 786436
  201.9 2.2 copy-start.3
  201.9 2.2 copy-start.4
  201.9 2.2 copy-start.6
  204.2 2.8 %copy-start.11 = (bf16[512,3584]{1,0:T(8,128)(2,1)S(1)}, bf16[512,3584]{1,0:T(8,128)(2,1)}, u32[]{:S(2)}) copy-start(bf16[512,3584]{1,0:T(8,128)(2,1)} %param.21) | copy-start | bytes 11010052
Sparse Core Ops, SparseCore 0:
  9.5 45.3 all-gather.10
  56.6 29.1 all-gather.6
  88.0 53.9 all-gather.4
  144.0 51.2 all-gather.8
  211.0 36.3 reduce-scatter.1
where the time goes:
time: 255 us; the launch traced here: 254 us
  waiting for transfers between devices  104 us (41%)
  blocking collectives  52.9 us (21%)
  matrix products  33.9 us (13%)
  local copies, waits for them, and re-layouts  21.9 us (9%)
  other arithmetic  17.3 us (7%)
  between operations  16.1 us (6%)
  starting transfers between devices  7.77 us (3%)
    reduce_scatter x1, waiting for transfers between devices, on_device(): lax.psum_scatter(partial_out.astype(jnp.bfloat16), 'mp', scatter_dimensio...  36.5 us
    all_gather x1, waiting for transfers between devices, on_device(): lax.all_gather(cached_rotated_keys, 'group', axis=0, tiled=True)  35.3 us
    all_gather x1, waiting for transfers between devices, on_device(): whole = lax.all_gather(stream, 'mp', axis=1, tiled=True)  28.5 us
    all_gather x1, blocking collectives, on_device(): lax.all_gather(adapter_down_rows, 'group', axis=0, tiled=True)  26.9 us
    psum x1, blocking collectives, on_device(): low = lax.psum(partial_low, 'mp').astype(jnp.bfloat16)  26 us
    ppermute x2, starting transfers between devices, shifted(): lax.ppermute(value, axis, [(source, source + steps) for source in range(f...  7.62 us
    unnamed x27, local copies, waits for them, and re-layouts  5.37 us
    dot_general x1, matrix products, on_device(): jnp.dot(normalized_input, query_weight, preferred_element_type=jnp.float32)  5.26 us
  transfers between devices with their start and end apart: 7, of which 4 were waited for; matrix products, arithmetic and copies ran while one was open for 22% of the time, Pallas kernels for 0%

commit v1 on v0

--- a/solution.py
+++ b/solution.py
@@ -118,7 +118,14 @@
     width = stream.shape[1]
     group_at = lax.axis_index("group")
     model_at = lax.axis_index("mp")
-    whole = lax.all_gather(stream, "mp", axis=1, tiled=True)
+    size = lax.axis_size("mp")
+    hops = [(i, (i + 1) % size) for i in range(size)]
+    parts = [stream]
+    for far in range(1, size):
+        parts = [lax.ppermute(parts[0], "mp", hops), *parts]
+    full = jnp.concatenate(parts, axis=1)
+    shift = (lax.axis_index("mp") + 1) * parts[-1].shape[1]
+    whole = jnp.roll(full, shift, axis=1)
     wide = whole.astype(jnp.float32)
     normalized_input = (
         wide * lax.rsqrt(jnp.mean(wide * wide, axis=1, keepdims=True) + 1e-06) * prenorm_gain

time: 255 us -> 243 us (0.953)
  waiting for transfers between devices: 104 us -> 77.8 us
  local copies, waits for them, and re-layouts: 21.9 us -> 36.1 us
    ppermute x0 -> x7, waiting for transfers between devices: none -> 40.8 us  [on_device(): parts = [lax.ppermute(parts[0], 'mp', hops), *parts]]
    all_gather x1, waiting for transfers between devices: 35.3 us -> 0.01 us  [on_device(): lax.all_gather(cached_rotated_keys, 'group', axis=0, tiled=True)]
    all_gather x1 -> x0, waiting for transfers between devices: 28.5 us -> none  [on_device(): whole = lax.all_gather(stream, 'mp', axis=1, tiled=True)]
    unnamed x27 -> x42, local copies, waits for them, and re-layouts: 5.37 us -> 18.8 us
    dot_general x1, matrix products: 3.76 us -> 1.16 us  [on_device(): jnp.dot(normalized_input, key_weight, preferred_element_type=jnp.float32)]
    dot_general x1, matrix products: 1.89 us -> 4.48 us  [on_device(): jnp.dot(normalized_input, value_weight, preferred_element_type=jnp.float32)]
  transfers between devices with their start and end apart: 7 -> 13, of which waited for: 4 -> 7; matrix products, arithmetic and copies ran while one was open for 22% -> 28% of each run, Pallas kernels for 0% -> 0%
where the time goes in v1:
time: 243 us; the launch traced here: 242 us
  waiting for transfers between devices  77.8 us (32%)
  blocking collectives  52.7 us (22%)
  local copies, waits for them, and re-layouts  36.1 us (15%)
  matrix products  35.6 us (15%)
  other arithmetic  17.3 us (7%)
  between operations  16.2 us (7%)
  starting transfers between devices  6.16 us (3%)
    ppermute x7, waiting for transfers between devices, on_device(): parts = [lax.ppermute(parts[0], 'mp', hops), *parts]  40.8 us
    reduce_scatter x1, waiting for transfers between devices, on_device(): lax.psum_scatter(partial_out.astype(jnp.bfloat16), 'mp', scatter_dimensio...  35 us
    all_gather x1, blocking collectives, on_device(): lax.all_gather(adapter_down_rows, 'group', axis=0, tiled=True)  27 us
    psum x1, blocking collectives, on_device(): low = lax.psum(partial_low, 'mp').astype(jnp.bfloat16)  25.7 us
    unnamed x42, local copies, waits for them, and re-layouts  18.8 us
    ppermute x2, starting transfers between devices, shifted(): lax.ppermute(value, axis, [(source, source + steps) for source in range(f...  5.99 us
    dot_general x1, matrix products, on_device(): jnp.dot(normalized_input, query_weight, preferred_element_type=jnp.float32)  5.26 us
  transfers between devices with their start and end apart: 13, of which 7 were waited for; matrix products, arithmetic and copies ran while one was open for 28% of the time, Pallas kernels for 0%

profile of v1, /device:TPU:0, one launch (start us, length us, event | category | flops | bytes accessed | tf_op | source)
XLA Modules:
  0.0 241.9 jit_solution(14970009428331778092)
XLA Ops:
  11.5 2.6 %compare_select_fusion.1 = s32[1024,1]{0,1:T(1,128)S(1)} fusion(s32[]{:T(128)} %bitcast.7, s32[]{:T(128)} %bitcast.8, s32[]{:T(128)} %bitcast.10, s32[]{:T(128)} %bitcast.9), kind=kLoop, calls=%fused_computation.87 | loop fusion | flops 17408 | bytes 4112 | tf_op jit(solution)/shard_map/gather | solution.py:75
  16.1 27.0 %all_gather.14 = bf16[64,16,448]{2,1,0:T(8,128)(2,1)S(1)} all-gather(bf16[4,16,448]{2,1,0:T(8,128)(2,1)} %param.22), channel_id=1, replica_groups=mesh['group'=16,'mp'=8] {'group'}, dimensions={0}, use_global_device_ids=true | all-gather | bytes 974848 | tf_op jit(solution)/shard_map/all_gather | solution.py:142
  48.3 4.0 %collective-permute-done.1 = bf16[512,448]{0,1:T(8,128)(2,1)} collective-permute-done((bf16[512,448]{0,1:T(8,128)(2,1)S(1)}, bf16[512,448]{0,1:T(8,128)(2,1)}, u32[]{:S(2)}, u32[]{:S(2)}) %collective-permute-start.1) | collective-permute-done | bytes 458784 | tf_op jit(solution)/shard_map/ppermute | solution.py:125
  54.2 7.5 %collective-permute-done.2 = bf16[512,448]{0,1:T(8,128)(2,1)S(1)} collective-permute-done((bf16[512,448]{0,1:T(8,128)(2,1)}, bf16[512,448]{0,1:T(8,128)(2,1)S(1)}, u32[]{:S(2)}, u32[]{:S(2)}) %collective-permute-start.2) | collective-permute-done | bytes 458784 | tf_op jit(solution)/shard_map/ppermute | solution.py:125
  63.2 7.6 %collective-permute-done.3 = bf16[512,448]{0,1:T(8,128)(2,1)} collective-permute-done((bf16[512,448]{0,1:T(8,128)(2,1)S(1)}, bf16[512,448]{0,1:T(8,128)(2,1)}, u32[]{:S(2)}, u32[]{:S(2)}) %collective-permute-start.3) | collective-permute-done | bytes 458784 | tf_op jit(solution)/shard_map/ppermute | solution.py:125
  73.4 6.9 %collective-permute-done.4 = bf16[512,448]{0,1:T(8,128)(2,1)} collective-permute-done((bf16[512,448]{0,1:T(8,128)(2,1)}, bf16[512,448]{0,1:T(8,128)(2,1)}, u32[]{:S(2)}, u32[]{:S(2)}) %collective-permute-start.4) | collective-permute-done | bytes 458784 | tf_op jit(solution)/shard_map/ppermute | solution.py:125
  81.8 7.9 %collective-permute-done.5 = bf16[512,448]{0,1:T(8,128)(2,1)} collective-permute-done((bf16[512,448]{0,1:T(8,128)(2,1)}, bf16[512,448]{0,1:T(8,128)(2,1)}, u32[]{:S(2)}, u32[]{:S(2)}) %collective-permute-start.5) | collective-permute-done | bytes 458784 | tf_op jit(solution)/shard_map/ppermute | solution.py:125
  89.8 2.5 %convolution_convert_fusion.2 = bf16[4,16,512]{2,0,1:T(4,128)(2,1)S(1)} fusion(bf16[64,16,512]{2,1,0:T(8,128)(2,1)} %all-gather.8.cloned.1.call-done, s32[4]{0:T(128)S(1)} %gather_fusion), kind=kOutput, calls=%fused_computation.28 | convolution fusion | flops 4227328 | bytes 1114128 | tf_op jit(solution)/shard_map/rj,jkd->rkd/dot_general | solution.py:148
  92.3 6.8 %collective-permute-done.6 = bf16[512,448]{0,1:T(8,128)(2,1)} collective-permute-done((bf16[512,448]{0,1:T(8,128)(2,1)}, bf16[512,448]{0,1:T(8,128)(2,1)}, u32[]{:S(2)}, u32[]{:S(2)}) %collective-permute-start.6) | collective-permute-done | bytes 458784 | tf_op jit(solution)/shard_map/ppermute | solution.py:125
  115.1 1.9 copy-done.1
  120.1 3.9 %collective-permute-start.8 = (bf16[512,256]{0,1:T(8,128)(2,1)}, bf16[512,256]{0,1:T(8,128)(2,1)}, u32[]{:S(2)}, u32[]{:S(2)}) collective-permute-start(bf16[512,256]{0,1:T(8,128)(2,1)} %maximum_bitcast_fusion.6), channel_id=1, source_target_pairs={{0,8},{8,16},{16,24},{24,32},{32,40},{40,48},{48,56},{56,64},{64,7... | collective-permute-start | bytes 786440 | tf_op jit(solution)/shard_map/ppermute | solution.py:14
  125.8 4.5 %convolution_convert_fusion.1 = bf16[512,256]{1,0:T(8,128)(2,1)} fusion(bf16[512,3584]{0,1:T(8,128)(2,1)} %copy-done.1, bf16[3584,256]{1,0:T(8,128)(2,1)} %param.20), kind=kOutput, calls=%fused_computation.27 | convolution fusion | flops 939655168 | bytes 5767168 | tf_op jit(solution)/shard_map/dot_general | solution.py:172
  130.3 2.1 collective-permute-start.7
  135.4 25.7 %all-reduce.1 = bf16[512,64]{0,1:T(8,128)(2,1)S(1)} all-reduce(f32[512,64]{0,1:T(8,128)S(1)} %bitcast.101), channel_id=1, replica_groups=mesh['group'=16,'mp'=8] {'mp'}, use_global_device_ids=true, to_apply=%region_5.6 | all-reduce | flops 32768 | bytes 196608 | tf_op jit(solution)/shard_map/psum | solution.py:155
  161.4 5.3 %convolution_add_fusion = f32[512,512]{0,1:T(8,128)S(1)} fusion(f32[512,512]{0,1:T(8,128)S(1)} %convolution_multiply_fusion, bf16[512,3584]{0,1:T(8,128)(2,1)} %copy-done.1, bf16[3584,512]{1,0:T(8,128)(2,1)} %param.18), kind=kOutput, calls=%fused_computation.23 | convolution fusion | flops 1879310336 | bytes 9437184 | tf_op jit(solution)/shard_map/dot_general | solution.py:163
  169.0 2.0 copy.63
  171.1 2.1 subtract_convert_fusion
  176.7 4.6 %fusion.20 = bf16[4,256,256]{2,0,1:T(4,128)(2,1)S(1)} fusion(bf16[32,256,256]{2,1,0:T(8,128)(2,1)} %all-gather.6.cloned.1.call-done, s32[4]{0:T(128)S(1)} %dynamic-slice_reduce_fusion.1), kind=kOutput, calls=%fused_computation.25 | convolution fusion | flops 17039488 | bytes 4718608 | tf_op jit(solution)/shard_map/rj,jcd->rcd/dot_general | solution.py:183
  182.2 4.6 %fusion.17 = bf16[4,256,256]{2,0,1:T(4,128)(2,1)S(1)} fusion(bf16[32,256,256]{2,1,0:T(8,128)(2,1)} %all-gather.4.cloned.1.call-done, s32[4]{0:T(128)S(1)} %dynamic-slice_reduce_fusion.1), kind=kOutput, calls=%fused_computation.24 | convolution fusion | flops 17039488 | bytes 4718608 | tf_op jit(solution)/shard_map/rj,jcd->rcd/dot_general | solution.py:184
  188.0 3.5 %fusion.5 = (f32[2,512]{1,0:T(2,128)S(1)}, f32[2048,512,2]{1,0,2:T(8,128)S(1)}) fusion(pred[512,2048]{0,1:T(8,128)(4,1)S(1)} %pad_add_fusion, bf16[512,2,128]{2,0,1:T(8,128)(2,1)} %get-tuple-element.13, bf16[512,2,128]{2,0,1:T(8,128)(2,1)} %get-tuple-element.12, bf16[512,256]{1,0:T(8,128)(2,1)} %copy.52, bf16[512,256]{1,0:T(8,128)(2,1)} %copy.51, ...), kind=kOutput, calls=%fused_computation.10 | convolution fusion | flops 1084226560 | bytes 11014144 | tf_op jit(solution)/shard_map/tkrd,skd->krts/dot_general | solution.py:82
  191.4 2.2 fusion
  193.7 2.8 %divide_convert_fusion = bf16[512,1,2,256]{0,3,2,1:T(8,128)(2,1)S(1)} fusion(f32[2048,512,2]{1,0,2:T(8,128)S(1)} %get-tuple-element.25, f32[2,512]{1,0:T(2,128)S(1)} %get-tuple-element.24, pred[512,2048]{0,1:T(8,128)(4,1)S(1)} %pad_add_fusion, bf16[512,256]{0,1:T(8,128)(2,1)S(1)} %copy-done.8, bf16[512,256]{0,1:T(8,128)(2,1)S(1)} %copy-done.9, ...), kind=kOutput, calls=%fused_computation.43 | convolution fusion | flops 1085800448 | bytes 11018240 | tf_op jit(solution)/shard_map/krts,skd->tkrd/dot_general | solution.py:89
  196.5 3.9 %convolution_convert_fusion = bf16[512,3584]{0,1:T(8,128)(2,1)} fusion(bf16[512,512]{0,1:T(8,128)(2,1)S(1)} %bitcast.107, bf16[512,3584]{1,0:T(8,128)(2,1)S(1)} %copy-done.11), kind=kOutput, calls=%fused_computation.11 | convolution fusion | flops 1880883200 | bytes 7864320 | tf_op jit(solution)/shard_map/dot_general | solution.py:201
  200.4 35.0 %reduce-scatter.2.cloned.1.call-done = bf16[512,448]{0,1:T(8,128)(2,1)} async-done(((bf16[512,3584]{0,1:T(8,128)(2,1)}), bf16[512,448]{0,1:T(8,128)(2,1)}) %reduce-scatter.2.cloned.1.call-update) | async-done | bytes 458768 | tf_op jit(solution)/shard_map/reduce_scatter | solution.py:202
  (105 shorter events, 48.8 us)
Async XLA Ops:
  6.5 110.5 %copy-start = (bf16[3584,256]{1,0:T(8,128)(2,1)S(1)}, bf16[3584,256]{1,0:T(8,128)(2,1)}, u32[]{:S(2)}) copy-start(bf16[3584,256]{1,0:T(8,128)(2,1)} %param.19) | copy-start | bytes 5505028
  6.5 83.3 %all-gather.8.cloned.1.call-start = ((), (), s32[]{:S(2)}) async-start(), calls=%async_computation.3 | async-start | bytes 1114112 | tf_op jit(solution)/shard_map/all_gather | solution.py:143
  7.3 169.5 %all-gather.6.cloned.1.call-start = ((), (), s32[]{:S(2)}) async-start(), calls=%async_computation.2 | async-start | bytes 4456448 | tf_op jit(solution)/shard_map/all_gather | solution.py:178
  8.0 174.2 %all-gather.4.cloned.1.call-start = ((), (), s32[]{:S(2)}) async-start(), calls=%async_computation.1 | async-start | bytes 4456448 | tf_op jit(solution)/shard_map/all_gather | solution.py:179
  8.1 35.0 %collective-permute-start = (bf16[512,448]{0,1:T(8,128)(2,1)}, bf16[512,448]{0,1:T(8,128)(2,1)S(1)}, u32[]{:S(2)}, u32[]{:S(2)}) collective-permute-start(bf16[512,448]{0,1:T(8,128)(2,1)} %param.16), channel_id=1, source_target_pairs={{0,1},{1,2},{2,3},{3,4},{4,5},{5,6},{6,7},{7,0},{8,9},{9,10},{10,1... | collective-permute-start | bytes 1376264 | tf_op jit(solution)/shard_map/ppermute | solution.py:125
  8.7 226.7 %reduce-scatter.2.cloned.1.call-start = ((), (), s32[]{:S(2)}) async-start(), calls=%async_computation.4 | async-start | bytes 4128768 | tf_op jit(solution)/shard_map/reduce_scatter | solution.py:202
  43.1 18.6 %copy-start.3 = (bf16[512,448]{0,1:T(8,128)(2,1)}, bf16[512,448]{0,1:T(8,128)(2,1)S(1)}, u32[]{:S(2)}) copy-start(bf16[512,448]{0,1:T(8,128)(2,1)S(1)} %collective-permute-done) | copy-start | bytes 1376260
  43.1 9.2 %collective-permute-start.1 = (bf16[512,448]{0,1:T(8,128)(2,1)S(1)}, bf16[512,448]{0,1:T(8,128)(2,1)}, u32[]{:S(2)}, u32[]{:S(2)}) collective-permute-start(bf16[512,448]{0,1:T(8,128)(2,1)S(1)} %collective-permute-done), channel_id=1, source_target_pairs={{0,1},{1,2},{2,3},{3,4},{4,5},{5,6},{6,7},{7,0},{8,9},{9,10},{10,1... | collective-permute-start | bytes 1376264 | tf_op jit(solution)/shard_map/ppermute | solution.py:125
  52.3 9.3 %collective-permute-start.2 = (bf16[512,448]{0,1:T(8,128)(2,1)}, bf16[512,448]{0,1:T(8,128)(2,1)S(1)}, u32[]{:S(2)}, u32[]{:S(2)}) collective-permute-start(bf16[512,448]{0,1:T(8,128)(2,1)} %collective-permute-done.1), channel_id=1, source_target_pairs={{0,1},{1,2},{2,3},{3,4},{4,5},{5,6},{6,7},{7,0},{8,9},{9,10},{10,1... | collective-permute-start | bytes 1376264 | tf_op jit(solution)/shard_map/ppermute | solution.py:125
  61.6 9.2 %collective-permute-start.3 = (bf16[512,448]{0,1:T(8,128)(2,1)S(1)}, bf16[512,448]{0,1:T(8,128)(2,1)}, u32[]{:S(2)}, u32[]{:S(2)}) collective-permute-start(bf16[512,448]{0,1:T(8,128)(2,1)S(1)} %collective-permute-done.2), channel_id=1, source_target_pairs={{0,1},{1,2},{2,3},{3,4},{4,5},{5,6},{6,7},{7,0},{8,9},{9,10},{10,1... | collective-permute-start | bytes 1376264 | tf_op jit(solution)/shard_map/ppermute | solution.py:125
  70.9 9.4 %collective-permute-start.4 = (bf16[512,448]{0,1:T(8,128)(2,1)}, bf16[512,448]{0,1:T(8,128)(2,1)}, u32[]{:S(2)}, u32[]{:S(2)}) collective-permute-start(bf16[512,448]{0,1:T(8,128)(2,1)} %collective-permute-done.3), channel_id=1, source_target_pairs={{0,1},{1,2},{2,3},{3,4},{4,5},{5,6},{6,7},{7,0},{8,9},{9,10},{10,1... | collective-permute-start | bytes 1376264 | tf_op jit(solution)/shard_map/ppermute | solution.py:125
  80.3 9.4 %collective-permute-start.5 = (bf16[512,448]{0,1:T(8,128)(2,1)}, bf16[512,448]{0,1:T(8,128)(2,1)}, u32[]{:S(2)}, u32[]{:S(2)}) collective-permute-start(bf16[512,448]{0,1:T(8,128)(2,1)} %collective-permute-done.4), channel_id=1, source_target_pairs={{0,1},{1,2},{2,3},{3,4},{4,5},{5,6},{6,7},{7,0},{8,9},{9,10},{10,1... | collective-permute-start | bytes 1376264 | tf_op jit(solution)/shard_map/ppermute | solution.py:125
  81.8 24.8 %copy-start.2 = (bf16[512,448]{0,1:T(8,128)(2,1)S(1)}, bf16[512,448]{0,1:T(8,128)(2,1)}, u32[]{:S(2)}) copy-start(bf16[512,448]{0,1:T(8,128)(2,1)} %param.16) | copy-start | bytes 1376260
  89.7 9.4 %collective-permute-start.6 = (bf16[512,448]{0,1:T(8,128)(2,1)}, bf16[512,448]{0,1:T(8,128)(2,1)}, u32[]{:S(2)}, u32[]{:S(2)}) collective-permute-start(bf16[512,448]{0,1:T(8,128)(2,1)} %collective-permute-done.5), channel_id=1, source_target_pairs={{0,1},{1,2},{2,3},{3,4},{4,5},{5,6},{6,7},{7,0},{8,9},{9,10},{10,1... | collective-permute-start | bytes 1376264 | tf_op jit(solution)/shard_map/ppermute | solution.py:125
  89.8 21.0 %copy-start.6 = (bf16[512,448]{0,1:T(8,128)(2,1)S(1)}, bf16[512,448]{0,1:T(8,128)(2,1)}, u32[]{:S(2)}) copy-start(bf16[512,448]{0,1:T(8,128)(2,1)} %copy-done.5) | copy-start | bytes 1376260
  89.8 22.1 %copy-start.4 = (bf16[512,448]{0,1:T(8,128)(2,1)S(1)}, bf16[512,448]{0,1:T(8,128)(2,1)}, u32[]{:S(2)}) copy-start(bf16[512,448]{0,1:T(8,128)(2,1)} %copy-done.3) | copy-start | bytes 1376260
  103.4 9.9 %copy-start.10 = (f32[3584]{0:T(1024)S(1)}, f32[3584]{0:T(1024)}, u32[]{:S(2)}) copy-start(f32[3584]{0:T(1024)} %param.17) | copy-start | bytes 43012
  115.1 1.9 copy-start.1
  120.1 53.1 %collective-permute-start.8 = (bf16[512,256]{0,1:T(8,128)(2,1)}, bf16[512,256]{0,1:T(8,128)(2,1)}, u32[]{:S(2)}, u32[]{:S(2)}) collective-permute-start(bf16[512,256]{0,1:T(8,128)(2,1)} %maximum_bitcast_fusion.6), channel_id=1, source_target_pairs={{0,8},{8,16},{16,24},{24,32},{32,40},{40,48},{48,56},{56,64},{64,7... | collective-permute-start | bytes 786440 | tf_op jit(solution)/shard_map/ppermute | solution.py:14
  130.3 44.7 %collective-permute-start.7 = (bf16[512,256]{1,0:T(8,128)(2,1)}, bf16[512,256]{1,0:T(8,128)(2,1)}, u32[]{:S(2)}, u32[]{:S(2)}) collective-permute-start(bf16[512,256]{1,0:T(8,128)(2,1)} %convolution_convert_fusion.1), channel_id=1, source_target_pairs={{0,8},{8,16},{16,24},{24,32},{32,40},{40,48},{48,56},{56,64},{64,7... | collective-permute-start | bytes 786440 | tf_op jit(solution)/shard_map/ppermute | solution.py:14
  191.4 2.2 copy-start.7
  191.4 2.2 copy-start.8
  191.4 2.2 copy-start.9
  193.7 2.8 %copy-start.11 = (bf16[512,3584]{1,0:T(8,128)(2,1)S(1)}, bf16[512,3584]{1,0:T(8,128)(2,1)}, u32[]{:S(2)}) copy-start(bf16[512,3584]{1,0:T(8,128)(2,1)} %param.21) | copy-start | bytes 11010052
  (1 other events, 0.8 us)
Sparse Core Ops, SparseCore 0:
  9.5 45.2 all-gather.7
  56.9 50.9 all-gather.5
  110.1 54.2 all-gather.3
  200.5 34.8 reduce-scatter.1
